TPU v7x, 128 devices: a whole 4x4x4 slice. The times are simulated.
128 devices in a mesh: dp: 2 (over core), seq: 16 (over z, x), head: 4 (over y).
Axes of the slice: x: 4, y: 4, z: 4, core: 2. Of those that a mesh axis runs over, the one named last changes fastest.
Arguments:
- queries: bfloat16 [2, 10240, 2048], P('dp', ('seq', 'head')), may hold values from -45 to 45
- key_rows: bfloat16 [2, 10240, 2048], P('dp', ('seq', 'head')), may hold values from -6 to 6
- values: bfloat16 [2, 10240, 2048], P('dp', ('seq', 'head')), may hold values from -6 to 6
- rand_blocks: int32 [160, 16, 4], P('seq', 'head'), may hold values from 0 to 159, as said below
- out_weight: bfloat16 [2048, 2048], P('head'), may hold values from -0.125 to 0.125
- cotangent: bfloat16 [2, 10240, 2048], P('dp', ('seq', 'head')), may hold values from -6 to 6
Outputs:
- layer_out: bfloat16 [2, 10240, 2048], P('dp', ('seq', 'head'))
- grad_queries: bfloat16 [2, 10240, 2048], P('dp', ('seq', 'head'))
- grad_keys: bfloat16 [2, 10240, 2048], P('dp', ('seq', 'head'))
- grad_values: bfloat16 [2, 10240, 2048], P('dp', ('seq', 'head'))
- weight_grad: float32 [2048, 2048], P('head')
Inputs may be any that keep to these rules, and one draw needn't show every extreme that they name: `rand_blocks`: key block b lies in range b // 10 of seq. Over the 10 query blocks of one index of seq and the 4 heads of one index of head, at most 15 of the listed random blocks lie in any one range of seq; in every draw, for every index of head, some range of seq receives exactly 15 of them from every index of seq.
All inputs are finite; a program needn't handle non-finite values.
Results may differ from a plain program's by a relative error of at most 0.034.
Values may be sent and summed in bfloat16 or wider, within the bound.
No kernel may reach another device: no remote copies, remote signals or barrier semaphores. Data moves between devices by JAX's collectives and lax.ppermute only.
A program may use at most 192 MiB of HBM per device.

v0:
```python
import math
import jax
import jax.numpy as jnp
from jax import lax
from jax.sharding import PartitionSpec as P

HEAD_SIZE = 128
BLOCK_TOKENS = 64


def with_halo(block, sides, width):
    for axis, dim in sides:
        count = lax.axis_size(axis)
        forward = [(i, i + 1) for i in range(count - 1)]
        backward = [(target, source) for source, target in forward]
        low = lax.ppermute(
            lax.slice_in_dim(block, block.shape[dim] - width, None, axis=dim), axis, forward
        )
        high = lax.ppermute(lax.slice_in_dim(block, 0, width, axis=dim), axis, backward)
        block = jnp.concatenate([low, block, high], axis=dim)
    return block


def from_root(block, axis, holder):
    block = jnp.where(lax.axis_index(axis) == holder, block, jnp.zeros_like(block))
    return lax.psum(block, axis)


def per_device(queries, key_rows, values, rand_blocks, out_weight, cotangent):
    block_len = BLOCK_TOKENS
    head_dim = HEAD_SIZE
    seq_count = lax.axis_size("seq")
    seq_index = lax.axis_index("seq")
    q_heads, k_heads, v_heads = (
        lax.all_to_all(queries, "head", split_axis=2, concat_axis=1, tiled=True),
        lax.all_to_all(key_rows, "head", split_axis=2, concat_axis=1, tiled=True),
        lax.all_to_all(values, "head", split_axis=2, concat_axis=1, tiled=True),
    )
    q_rows = q_heads[0]
    shard_len = q_rows.shape[0]
    width_cols = q_rows.shape[1]
    head_count = width_cols // head_dim
    block_count = shard_len // block_len
    rand_count = rand_blocks.shape[2]
    key_value = jnp.concatenate([k_heads[0], v_heads[0]], axis=1)
    padded = with_halo(key_value, (("seq", 0),), block_len)
    first_block = from_root(key_value[:block_len], "seq", 0)
    requests = jnp.transpose(rand_blocks, (0, 2, 1)).reshape(-1)
    request_count = requests.shape[0]
    head_of = jnp.arange(request_count, dtype=jnp.int32) % head_count
    capacity = 3 * request_count // (2 * seq_count)
    owners = requests // block_count
    offsets = requests % block_count
    one_hot = (owners[:, None] == jnp.arange(seq_count, dtype=jnp.int32)[None, :]).astype(jnp.int32)
    position = jnp.sum(one_hot * (jnp.cumsum(one_hot, axis=0) - 1), axis=1)
    slot_of = owners * capacity + position
    asked_codes = (
        jnp.full((seq_count * capacity,), -1, jnp.int32)
        .at[slot_of]
        .set(offsets * head_count + head_of)
        .reshape(seq_count, capacity)
    )
    asked_here = lax.all_to_all(asked_codes, "seq", split_axis=0, concat_axis=0, tiled=True)
    is_valid = asked_here >= 0
    asked_block = jnp.maximum(asked_here, 0) // head_count
    asked_head = jnp.maximum(asked_here, 0) % head_count
    block_view = key_value.reshape(block_count, block_len, 2, head_count, head_dim)
    served = block_view[asked_block, :, :, asked_head, :]
    served = jnp.where(is_valid[:, :, None, None, None], served, jnp.zeros_like(served))
    served = served.reshape(seq_count, capacity, block_len, 2 * head_dim)
    received = lax.all_to_all(served, "seq", split_axis=0, concat_axis=0, tiled=True)
    far_pairs = received.reshape(seq_count * capacity, block_len, 2, head_dim)[slot_of]
    pair_view = padded.reshape(block_count + 2, block_len, 2, head_count, head_dim)
    window_pairs = jnp.stack(
        [pair_view[:block_count], pair_view[1 : block_count + 1], pair_view[2:]], axis=1
    ).reshape(block_count, 3 * block_len, 2, head_count, head_dim)
    window_keys = window_pairs[:, :, 0]
    window_vals = window_pairs[:, :, 1]
    first_pairs = first_block.reshape(block_len, 2, head_count, head_dim)
    first_keys = first_pairs[:, 0]
    first_vals = first_pairs[:, 1]
    far_view = far_pairs.reshape(block_count, rand_count, head_count, block_len, 2, head_dim)
    far_keys = far_view[:, :, :, :, 0]
    far_vals = far_view[:, :, :, :, 1]
    global_ids = seq_index * block_count + jnp.arange(block_count, dtype=jnp.int32)
    block_total = seq_count * block_count
    window_live = jnp.stack([global_ids > 0, global_ids >= 0, global_ids < block_total - 1], axis=1)
    window_mask = jnp.repeat(window_live, block_len, axis=1)[None, :, None, :]
    query_blocks = q_rows.reshape(block_count, block_len, head_count, head_dim)
    softmax_scale = 1.0 / math.sqrt(head_dim)
    score_window = (
        jnp.einsum("ibhd,ikhd->hibk", query_blocks, window_keys, preferred_element_type=jnp.float32)
        * softmax_scale
    )
    score_first = (
        jnp.einsum("ibhd,khd->hibk", query_blocks, first_keys, preferred_element_type=jnp.float32)
        * softmax_scale
    )
    score_far = (
        jnp.einsum("ibhd,irhtd->hibrt", query_blocks, far_keys, preferred_element_type=jnp.float32)
        * softmax_scale
    )
    max_window = jnp.max(jnp.where(window_mask, score_window, -jnp.inf), axis=-1, keepdims=True)
    max_first = jnp.max(score_first, axis=-1, keepdims=True)
    max_far = jnp.max(score_far, axis=(-2, -1))[..., None]
    row_max = jnp.maximum(jnp.maximum(max_window, max_first), max_far)
    weight_window = jnp.where(window_mask, jnp.exp(score_window - row_max), 0.0)
    weight_first = jnp.exp(score_first - row_max)
    weight_far = jnp.exp(score_far - row_max[..., None])
    totals = (
        jnp.sum(weight_window, axis=-1, keepdims=True)
        + jnp.sum(weight_first, axis=-1, keepdims=True)
        + jnp.sum(weight_far, axis=(-2, -1))[..., None]
    )
    mixed = jnp.einsum(
        "hibk,ikhd->ibhd",
        weight_window.astype(jnp.bfloat16),
        window_vals,
        preferred_element_type=jnp.float32,
    )
    mixed = mixed + jnp.einsum(
        "hibk,khd->ibhd",
        weight_first.astype(jnp.bfloat16),
        first_vals,
        preferred_element_type=jnp.float32,
    )
    mixed = mixed + jnp.einsum(
        "hibrt,irhtd->ibhd",
        weight_far.astype(jnp.bfloat16),
        far_vals,
        preferred_element_type=jnp.float32,
    )
    totals_rows = jnp.transpose(totals, (1, 2, 0, 3))
    attn = (mixed / totals_rows).astype(jnp.bfloat16)
    logsum = row_max + jnp.log(totals)
    attn_rows = attn.reshape(shard_len, width_cols)
    layer_out = lax.psum_scatter(
        jnp.dot(attn_rows, out_weight, preferred_element_type=jnp.float32),
        "head",
        scatter_dimension=0,
        tiled=True,
    ).astype(jnp.bfloat16)[None]
    piece_flat = lax.all_gather(cotangent, "head", axis=1, tiled=True)[0]
    grad_piece = jnp.dot(piece_flat, out_weight.T, preferred_element_type=jnp.float32).astype(
        jnp.bfloat16
    )
    weight_acc = jnp.dot(attn_rows.T, piece_flat, preferred_element_type=jnp.float32)
    token_total = lax.axis_size("dp") * seq_count * shard_len
    weight_grad = lax.psum(weight_acc, ("dp", "seq")) * (1.0 / math.sqrt(token_total))
    grad_blocks = grad_piece.reshape(block_count, block_len, head_count, head_dim)
    delta_rows = jnp.sum(grad_blocks.astype(jnp.float32) * attn.astype(jnp.float32), axis=-1)
    row_delta = jnp.transpose(delta_rows, (2, 0, 1))[..., None]
    prob_window = jnp.where(window_mask, jnp.exp(score_window - logsum), 0.0)
    prob_first = jnp.exp(score_first - logsum)
    prob_far = jnp.exp(score_far - logsum[..., None])
    dprob_window = jnp.einsum(
        "ibhd,ikhd->hibk", grad_blocks, window_vals, preferred_element_type=jnp.float32
    )
    dprob_first = jnp.einsum(
        "ibhd,khd->hibk", grad_blocks, first_vals, preferred_element_type=jnp.float32
    )
    dprob_far = jnp.einsum(
        "ibhd,irhtd->hibrt", grad_blocks, far_vals, preferred_element_type=jnp.float32
    )
    dscore_window = (prob_window * (dprob_window - row_delta)).astype(jnp.bfloat16)
    dscore_first = (prob_first * (dprob_first - row_delta)).astype(jnp.bfloat16)
    dscore_far = (prob_far * (dprob_far - row_delta[..., None])).astype(jnp.bfloat16)
    grad_q = jnp.einsum(
        "hibk,ikhd->ibhd", dscore_window, window_keys, preferred_element_type=jnp.float32
    )
    grad_q = grad_q + jnp.einsum(
        "hibk,khd->ibhd", dscore_first, first_keys, preferred_element_type=jnp.float32
    )
    grad_q = grad_q + jnp.einsum(
        "hibrt,irhtd->ibhd", dscore_far, far_keys, preferred_element_type=jnp.float32
    )
    grad_q = (grad_q * softmax_scale).astype(jnp.bfloat16)
    key_window = (
        jnp.einsum(
            "hibk,ibhd->ikhd", dscore_window, query_blocks, preferred_element_type=jnp.float32
        )
        * softmax_scale
    )
    value_window = jnp.einsum(
        "hibk,ibhd->ikhd",
        prob_window.astype(jnp.bfloat16),
        grad_blocks,
        preferred_element_type=jnp.float32,
    )
    key_first = (
        jnp.einsum("hibk,ibhd->khd", dscore_first, query_blocks, preferred_element_type=jnp.float32)
        * softmax_scale
    )
    value_first = jnp.einsum(
        "hibk,ibhd->khd",
        prob_first.astype(jnp.bfloat16),
        grad_blocks,
        preferred_element_type=jnp.float32,
    )
    key_far = (
        jnp.einsum(
            "hibrt,ibhd->irhtd", dscore_far, query_blocks, preferred_element_type=jnp.float32
        )
        * softmax_scale
    )
    value_far = jnp.einsum(
        "hibrt,ibhd->irhtd",
        prob_far.astype(jnp.bfloat16),
        grad_blocks,
        preferred_element_type=jnp.float32,
    )
    window_terms = jnp.stack(
        [
            key_window.reshape(block_count, 3, block_len, head_count, head_dim),
            value_window.reshape(block_count, 3, block_len, head_count, head_dim),
        ],
        axis=3,
    )
    grad_pad = jnp.zeros((block_count + 2, block_len, 2, head_count, head_dim), jnp.float32)
    grad_pad = (
        grad_pad.at[:block_count]
        .add(window_terms[:, 0])
        .at[1 : block_count + 1]
        .add(window_terms[:, 1])
        .at[2:]
        .add(window_terms[:, 2])
    )
    global_grad = lax.psum(jnp.stack([key_first, value_first], axis=1), "seq")
    grad_pad = grad_pad.at[1].add(jnp.where(seq_index == 0, global_grad, 0.0))
    rims = jnp.concatenate([grad_pad[0], grad_pad[block_count + 1]], axis=0).reshape(
        2 * block_len, 2 * width_cols
    )
    rim_sums = with_halo(rims.astype(jnp.bfloat16), (("seq", 0),), block_len).astype(rims.dtype)
    core = grad_pad[1 : block_count + 1].reshape(shard_len, 2 * width_cols)
    core = (
        core.at[:block_len]
        .add(rim_sums[:block_len])
        .at[shard_len - block_len :]
        .add(rim_sums[3 * block_len :])
    )
    core = core.reshape(block_count, block_len, 2, head_count, head_dim)
    far_terms = (
        jnp.stack([key_far, value_far], axis=4)
        .reshape(request_count, block_len, 2, head_dim)
        .astype(jnp.bfloat16)
    )
    outgoing = (
        jnp.zeros((seq_count * capacity, block_len, 2, head_dim), jnp.bfloat16)
        .at[slot_of]
        .set(far_terms)
    )
    outgoing = outgoing.reshape(seq_count, capacity, block_len, 2 * head_dim)
    incoming = (
        lax.all_to_all(outgoing, "seq", split_axis=0, concat_axis=0, tiled=True)
        .reshape(seq_count, capacity, block_len, 2, head_dim)
        .astype(jnp.float32)
    )
    incoming = jnp.where(is_valid[:, :, None, None, None], incoming, 0.0)
    core = core.at[asked_block, :, :, asked_head, :].add(incoming)
    grad_k = core[:, :, 0].reshape(shard_len, width_cols).astype(jnp.bfloat16)
    grad_v = core[:, :, 1].reshape(shard_len, width_cols).astype(jnp.bfloat16)
    grad_q_rows = grad_q.reshape(shard_len, width_cols)
    grad_queries, grad_keys, grad_values = (
        lax.all_to_all(grad_q_rows[None], "head", split_axis=1, concat_axis=2, tiled=True),
        lax.all_to_all(grad_k[None], "head", split_axis=1, concat_axis=2, tiled=True),
        lax.all_to_all(grad_v[None], "head", split_axis=1, concat_axis=2, tiled=True),
    )
    return (layer_out, grad_queries, grad_keys, grad_values, weight_grad)


def solution(mesh):
    in_specs = (
        P("dp", ("seq", "head"), None),
        P("dp", ("seq", "head"), None),
        P("dp", ("seq", "head"), None),
        P("seq", "head", None),
        P("head", None),
        P("dp", ("seq", "head"), None),
    )
    out_specs = (
        P("dp", ("seq", "head"), None),
        P("dp", ("seq", "head"), None),
        P("dp", ("seq", "head"), None),
        P("dp", ("seq", "head"), None),
        P("head", None),
    )
    return jax.shard_map(
        per_device, mesh=mesh, in_specs=in_specs, out_specs=out_specs, check_vma=False
    )
```

profile of v0, /device:TPU:38, one launch (start us, length us, event | category | flops | bytes accessed | tf_op | source)
XLA Modules:
  0.0 795.5 jit_solution(17635221475031465558)
XLA Ops:
  13.4 7.8 all-to-all-start.3
  21.2 5.9 copy.314
  27.6 12.6 %reduce.16 = bf16[2048,160]{1,0:T(8,128)(2,1)S(1)} reduce(bf16[2048,1,160]{2,1,0:T(2,128)(2,1)} %bitcast.313, bf16[]{:T(256)} %broadcast.542), dimensions={1}, to_apply=%bitcast.270.reduce_sub_computation | reduce | bytes 1310722
  42.5 4.5 all-to-all-start.1
  47.0 5.9 copy.311
  52.8 12.6 %reduce.17 = bf16[2048,160]{1,0:T(8,128)(2,1)S(1)} reduce(bf16[2048,1,160]{2,1,0:T(2,128)(2,1)} %bitcast.317, bf16[]{:T(256)} %broadcast.542), dimensions={1}, to_apply=%bitcast.272.reduce_sub_computation | reduce | bytes 1310722
  67.8 5.1 all-to-all-start
  72.9 5.9 copy.319
  78.7 12.6 %reduce.15 = bf16[2048,160]{1,0:T(8,128)(2,1)S(1)} reduce(bf16[2048,1,160]{2,1,0:T(2,128)(2,1)} %bitcast.318, bf16[]{:T(256)} %broadcast.542), dimensions={1}, to_apply=%bitcast.274.reduce_sub_computation | reduce | bytes 1310722
  94.3 4.2 reshape.654
  98.6 4.5 copy.315
  103.7 4.8 all-to-all-start.2
  108.5 4.2 reshape.656
  112.7 5.7 copy.312
  120.7 3.4 collective-permute-start
  127.5 5.5 collective-permute-done.1
  133.0 5.4 pad_maximum_fusion.6
  143.0 12.1 %gather_fusion = bf16[240,64,2,128]{3,1,2,0:T(8,128)(2,1)} fusion(bf16[10,64,2,4,128]{4,1,3,2,0:T(8,128)(2,1)S(1)} %copy.335, s32[240]{0:T(256)S(1)} %reshape.602), kind=kCustom, calls=%fused_computation | custom fusion | bytes 15730560 | tf_op jit(solution)/shard_map/gather | solution.py:68
  155.1 15.3 %copy.336 = bf16[240,64,2,128]{3,2,1,0:T(2,128)(2,1)} copy(bf16[240,64,2,128]{3,1,2,0:T(8,128)(2,1)} %gather_fusion) | data formatting | bytes 15728640 | tf_op jit(solution)/shard_map/gather | solution.py:68
  170.4 13.4 %gather.9 = bf16[16,15,64,256]{3,2,1,0:T(8,128)(2,1)} reshape(bf16[240,64,2,128]{3,2,1,0:T(2,128)(2,1)} %copy.336) | data formatting | bytes 15728640 | tf_op jit(solution)/shard_map/gather | solution.py:68
  183.8 7.0 broadcast_select_fusion.1
  190.8 6.7 all-to-all-start.4
  199.5 4.2 reshape.658
  203.7 5.7 copy.320
  218.4 3.9 stack.41
  224.1 5.0 pad_maximum_fusion.1
  232.1 108.2 %all-reduce.6.cloned.1.call-done = bf16[64,2,4,128]{3,0,2,1:T(8,128)(2,1)} async-done(((bf16[64,2,4,128]{3,0,2,1:T(8,128)(2,1)}), bf16[64,2,4,128]{3,0,2,1:T(8,128)(2,1)}) %all-reduce.6.cloned.1.call-update) | async-done | bytes 131088 | tf_op jit(solution)/shard_map/psum | solution.py:26
  343.0 4.7 select_reduce_fusion
  350.0 4.1 fusion.66
  355.8 12.2 %reshape.589 = bf16[240,64,2,128]{3,2,1,0:T(2,128)(2,1)} reshape(bf16[16,15,64,256]{3,2,1,0:T(8,128)(2,1)} %all-to-all-done.4) | data formatting | bytes 15728640 | tf_op jit(solution)/shard_map/reshape | solution.py:72
  368.0 8.5 %copy.337 = bf16[240,64,2,128]{3,1,2,0:T(8,128)(2,1)} copy(bf16[240,64,2,128]{3,2,1,0:T(2,128)(2,1)} %reshape.589) | data formatting | bytes 15728640 | tf_op jit(solution)/shard_map/reshape | solution.py:72
  376.5 11.2 %gather_fusion.1 = bf16[160,64,2,128]{3,1,2,0:T(8,128)(2,1)} fusion(bf16[240,64,2,128]{3,1,2,0:T(8,128)(2,1)} %copy.337, s32[1024]{0:T(1024)S(1)} %pad_clamp_fusion), kind=kCustom, calls=%fused_computation.1 | custom fusion | bytes 10486400 | tf_op jit(solution)/shard_map/gather | solution.py:72
  387.7 7.3 slice_bitcast_fusion.5
  418.5 3.9 fusion.17
  422.4 3.3 convert_bitcast_fusion
  433.2 4.2 copy.383
  437.4 5.1 broadcast_in_dim.101
  442.5 24.2 %scatter_fusion = bf16[240,64,2,128]{3,1,2,0:T(8,128)(2,1)} fusion(bf16[240,64,2,128]{3,1,2,0:T(8,128)(2,1)} %broadcast_in_dim.101, s32[160]{0:T(256)S(1)} %bitcast.345, bf16[160,64,2,128]{3,1,2,0:T(8,128)(2,1)} %copy.383), kind=kCustom, calls=%fused_computation.3 | custom fusion | bytes 15729280 | tf_op jit(solution)/shard_map/scatter | solution.py:250
  466.7 15.4 %copy.384 = bf16[240,64,2,128]{3,2,1,0:T(2,128)(2,1)} copy(bf16[240,64,2,128]{3,1,2,0:T(8,128)(2,1)} %scatter_fusion) | data formatting | bytes 15728640 | tf_op jit(solution)/shard_map/scatter | solution.py:250
  482.1 13.4 %reshape.599 = bf16[16,15,64,256]{3,2,1,0:T(8,128)(2,1)} reshape(bf16[240,64,2,128]{3,2,1,0:T(2,128)(2,1)} %copy.384) | data formatting | bytes 15728640 | tf_op jit(solution)/shard_map/reshape | solution.py:252
  495.5 7.2 all-to-all-start.6
  502.7 3.8 fusion.85
  522.0 3.8 fusion.14
  525.7 3.8 fusion.8
  536.7 5.2 collective-permute-start.2
  541.9 3.6 fusion.63
  548.5 5.5 reduce.18
  560.6 4.2 reshape.596
  565.0 38.2 %collective-permute-done.3 = bf16[64,1024]{1,0:T(8,128)(2,1)S(1)} collective-permute-done((bf16[64,1024]{1,0:T(8,128)(2,1)S(1)}, bf16[64,1024]{1,0:T(8,128)(2,1)S(1)}, u32[]{:S(2)}, u32[]{:S(2)}) %collective-permute-start.3) | collective-permute-done | bytes 131104 | tf_op jit(solution)/shard_map/ppermute | solution.py:19
  603.2 20.1 %collective-permute-done.2 = bf16[64,1024]{1,0:T(8,128)(2,1)S(1)} collective-permute-done((bf16[64,1024]{1,0:T(8,128)(2,1)S(1)}, bf16[64,1024]{1,0:T(8,128)(2,1)S(1)}, u32[]{:S(2)}, u32[]{:S(2)}) %collective-permute-start.2) | collective-permute-done | bytes 131104 | tf_op jit(solution)/shard_map/ppermute | solution.py:16
  625.7 4.2 reshape.598
  629.9 3.7 copy.385
  633.6 4.8 all-to-all-start.5
  638.4 16.2 %reshape.601 = f32[16,15,64,2,128]{4,3,2,1,0:T(2,128)} reshape(bf16[16,15,64,256]{3,2,1,0:T(8,128)(2,1)} %all-to-all-done.6) | data formatting | bytes 23592960 | tf_op jit(solution)/shard_map/convert_element_type | solution.py:256
  654.6 12.1 %broadcast_select_fusion = f32[16,15,64,2,128]{4,3,2,1,0:T(2,128)} fusion(f32[16,15,64,2,128]{4,3,2,1,0:T(2,128)} %reshape.601, pred[16,15]{1,0:T(8,128)(4,1)S(1)} %compare_bitcast_fusion), kind=kLoop, calls=%fused_computation.5 | loop fusion | flops 3932160 | bytes 31457520 | tf_op jit(solution)/shard_map/jit(_where)/select_n | solution.py:258
  666.8 13.5 %copy.386 = f32[240,64,2,128]{3,1,2,0:T(8,128)} copy(f32[240,64,2,128]{3,2,1,0:T(2,128)} %bitcast.298) | data formatting | bytes 31457280 | tf_op jit(solution)/shard_map/jit(_where)/select_n | solution.py:258
  680.3 50.5 %scatter_fusion.1 = f32[10,64,2,4,128]{4,1,3,2,0:T(8,128)} fusion(f32[10,64,2,4,128]{4,1,3,2,0:T(8,128)} %copy.385, s32[240]{0:T(256)S(1)} %reshape.632, f32[240,64,2,128]{3,1,2,0:T(8,128)} %copy.386), kind=kCustom, calls=%fused_computation.4 | custom fusion | flops 3932160 | bytes 47187840 | tf_op jit(solution)/shard_map/scatter-add | solution.py:259
  735.1 3.7 convert_element_type.101
  738.8 5.4 reduce.19
  747.1 4.9 all-to-all-start.7
  756.8 3.7 convert_element_type.102
  760.5 5.4 reduce.20
  768.8 4.8 all-to-all-start.8
  773.6 5.0 broadcast_multiply_fusion
  (218 shorter events, 136.9 us)
Async XLA Ops:
  8.0 342.0 %copy-start = (bf16[512,2048]{1,0:T(8,128)(2,1)S(1)}, bf16[512,2048]{1,0:T(8,128)(2,1)}, u32[]{:S(2)}) copy-start(bf16[512,2048]{1,0:T(8,128)(2,1)} %param.22) | copy-start | bytes 6291460
  11.6 15.5 %copy-start.31 = (s32[160,1]{0,1:T(1,128)}, s32[160,1]{0,1:T(1,128)S(1)}, u32[]{:S(2)}) copy-start(s32[160,1]{0,1:T(1,128)S(1)} %compare_select_fusion.2) | copy-start | bytes 1924
  13.4 29.1 %all-to-all-start.3 = ((s32[16,1,15]{2,1,0:T(1,128)}), s32[16,1,15]{2,1,0:T(1,128)S(1)}, u32[]{:S(2)}, u32[]{:S(2)}) async-start(s32[16,1,15]{2,1,0:T(1,128)} %bitcast.19), calls=%async_computation.3 | async-start | bytes 16384 | tf_op jit(solution)/shard_map/all_to_all | solution.py:63
  42.5 25.2 %all-to-all-start.1 = ((bf16[4,2,40960]{2,1,0:T(2,128)(2,1)}), bf16[4,2,40960]{2,1,0:T(2,128)(2,1)}, u32[]{:S(2)}, u32[]{:S(2)}) async-start(bf16[4,2,40960]{2,1,0:T(2,128)(2,1)} %reshape.653), calls=%async_computation.1 | async-start | bytes 1310720 | tf_op jit(solution)/shard_map/all_to_all | solution.py:37
  67.8 35.9 %all-to-all-start = ((bf16[4,2,40960]{2,1,0:T(2,128)(2,1)}), bf16[4,2,40960]{2,1,0:T(2,128)(2,1)}, u32[]{:S(2)}, u32[]{:S(2)}) async-start(bf16[4,2,40960]{2,1,0:T(2,128)(2,1)} %reshape.655), calls=%async_computation | async-start | bytes 1310720 | tf_op jit(solution)/shard_map/all_to_all | solution.py:36
  103.7 17.0 %copy-start.20 = (bf16[1,4,160,512]{3,2,1,0:T(8,128)(2,1)}, bf16[1,4,160,512]{3,2,1,0:T(8,128)(2,1)S(1)}, u32[]{:S(2)}) copy-start(bf16[1,4,160,512]{3,2,1,0:T(8,128)(2,1)S(1)} %copy.316) | copy-start | bytes 1966084
  103.7 87.1 %all-to-all-start.2 = ((bf16[4,2,40960]{2,1,0:T(2,128)(2,1)}), bf16[4,2,40960]{2,1,0:T(2,128)(2,1)}, u32[]{:S(2)}, u32[]{:S(2)}) async-start(bf16[4,2,40960]{2,1,0:T(2,128)(2,1)} %reshape.657), calls=%async_computation.2 | async-start | bytes 1310720 | tf_op jit(solution)/shard_map/all_to_all | solution.py:35
  120.7 6.9 collective-permute-start
  124.0 9.0 %collective-permute-start.1 = (bf16[64,1024]{1,0:T(8,128)(2,1)S(1)}, bf16[64,1024]{1,0:T(8,128)(2,1)S(1)}, u32[]{:S(2)}, u32[]{:S(2)}) collective-permute-start(bf16[64,1024]{1,0:T(8,128)(2,1)S(1)} %get-tuple-element.80), channel_id=1, source_target_pairs={{4,0},{8,4},{12,8},{16,12},{20,16},{24,20},{28,24},{32,28},{36,32}... | collective-permute-start | bytes 393224 | tf_op jit(solution)/shard_map/ppermute | solution.py:19
  138.4 1.1 copy-start.8
  190.8 8.7 %copy-start.32 = (s32[160,1]{0,1:T(1,128)S(1)}, s32[160,1]{0,1:T(1,128)}, u32[]{:S(2)}) copy-start(s32[160,1]{0,1:T(1,128)} %copy-done.31) | copy-start | bytes 1924
  190.8 165.0 %all-to-all-start.4 = ((bf16[16,15,64,256]{3,2,1,0:T(8,128)(2,1)}), bf16[16,15,64,256]{3,2,1,0:T(8,128)(2,1)}, u32[]{:S(2)}, u32[]{:S(2)}) async-start(bf16[16,15,64,256]{3,2,1,0:T(8,128)(2,1)} %broadcast_select_fusion.1), calls=%async_computation.4 | async-start | bytes 15728640 | tf_op jit(solution)/shard_map/all_to_all | solution.py:71
  197.5 142.8 %all-reduce.6.cloned.1.call-start = ((), (), s32[]{:S(2)}) async-start(), calls=%async_computation.10 | async-start | bytes 262144 | tf_op jit(solution)/shard_map/psum | solution.py:26
  198.4 151.7 %all-gather.2.cloned.1.call-start = ((), (), s32[]{:S(2)}) async-start(), calls=%async_computation.12 | async-start | bytes 3276800 | tf_op jit(solution)/shard_map/all_gather | solution.py:143
  198.9 330.6 %all-reduce.8.cloned.1.call-start = ((), (), s32[]{:S(2)}) async-start(), calls=%async_computation.13 | async-start | bytes 524288 | tf_op jit(solution)/shard_map/psum | solution.py:228
  209.4 7.2 copy-start.9
  218.4 3.9 copy-start.21
  229.0 111.3 %copy-start.10 = (bf16[10,64,4,128]{3,2,1,0:T(4,128)(2,1)S(1)}, bf16[10,64,4,128]{3,2,1,0:T(4,128)(2,1)}, u32[]{:S(2)}) copy-start(bf16[10,64,4,128]{3,2,1,0:T(4,128)(2,1)} %reshape_squeeze.2) | copy-start | bytes 1966084
  343.0 4.7 copy-start.6
  355.8 59.4 %copy-start.2 = (bf16[10,64,4,128]{3,2,1,0:T(4,128)(2,1)}, bf16[10,64,4,128]{3,2,1,0:T(4,128)(2,1)S(1)}, u32[]{:S(2)}) copy-start(bf16[10,64,4,128]{3,2,1,0:T(4,128)(2,1)S(1)} %reshape.592) | copy-start | bytes 1966084
  395.9 6.9 copy-start.1
  396.0 3.6 copy-start.13
  397.4 3.2 copy-start.5
  405.9 1.0 copy-start.28
  405.9 1.6 copy-start.27
  411.3 0.8 copy-start.25
  412.9 360.7 %all-reduce.10.cloned.1.call-start = ((), (), s32[]{:S(2)}) async-start(), calls=%async_computation.14 | async-start | bytes 8388608 | tf_op jit(solution)/shard_map/psum | solution.py:149
  415.2 3.2 copy-start.18
  415.3 3.2 copy-start.23
  422.4 4.0 slice-start
  422.4 4.1 slice-start.1
  425.7 1.3 copy-start.3
  425.7 2.1 copy-start.17
  427.9 3.2 copy-start.11
  429.6 1.5 copy-start.14
  495.5 7.2 copy-start.19
  495.5 138.2 %all-to-all-start.6 = ((bf16[16,15,64,256]{3,2,1,0:T(8,128)(2,1)}), bf16[16,15,64,256]{3,2,1,0:T(8,128)(2,1)}, u32[]{:S(2)}, u32[]{:S(2)}) async-start(bf16[16,15,64,256]{3,2,1,0:T(8,128)(2,1)} %reshape.599), calls=%async_computation.7 | async-start | bytes 15728640 | tf_op jit(solution)/shard_map/all_to_all | solution.py:254
  502.6 283.3 %reduce-scatter.2.cloned.1.call-start = ((), (), s32[]{:S(2)}) async-start(), calls=%async_computation.11 | async-start | bytes 6553600 | tf_op jit(solution)/shard_map/reduce_scatter | solution.py:137
  506.5 0.7 copy-start.30
  506.5 1.1 copy-start.4
  507.6 2.5 copy-start.7
  510.1 3.0 copy-start.12
  513.2 1.1 copy-start.22
  515.1 2.3 copy-start.26
  515.3 2.1 copy-start.29
  515.3 3.5 copy-start.15
  515.3 4.5 copy-start.16
  533.7 69.5 %collective-permute-start.3 = (bf16[64,1024]{1,0:T(8,128)(2,1)S(1)}, bf16[64,1024]{1,0:T(8,128)(2,1)S(1)}, u32[]{:S(2)}, u32[]{:S(2)}) collective-permute-start(bf16[64,1024]{1,0:T(8,128)(2,1)S(1)} %concatenate.44), channel_id=1, source_target_pairs={{4,0},{8,4},{12,8},{16,12},{20,16},{24,20},{28,24},{32,28},{36,32}... | collective-permute-start | bytes 393224 | tf_op jit(solution)/shard_map/ppermute | solution.py:19
  536.7 86.6 %collective-permute-start.2 = (bf16[64,1024]{1,0:T(8,128)(2,1)S(1)}, bf16[64,1024]{1,0:T(8,128)(2,1)S(1)}, u32[]{:S(2)}, u32[]{:S(2)}) collective-permute-start(bf16[64,1024]{1,0:T(8,128)(2,1)S(1)} %concatenate.43), channel_id=1, source_target_pairs={{0,4},{4,8},{8,12},{12,16},{16,20},{20,24},{24,28},{28,32},{32,36}... | collective-permute-start | bytes 393224 | tf_op jit(solution)/shard_map/ppermute | solution.py:16
  633.6 113.5 %all-to-all-start.5 = ((bf16[4,2,40960]{2,1,0:T(2,128)(2,1)}), bf16[4,2,40960]{2,1,0:T(2,128)(2,1)}, u32[]{:S(2)}, u32[]{:S(2)}) async-start(bf16[4,2,40960]{2,1,0:T(2,128)(2,1)} %reshape.659), calls=%async_computation.6 | async-start | bytes 1310720 | tf_op jit(solution)/shard_map/all_to_all | solution.py:264
  747.1 21.7 %all-to-all-start.7 = ((bf16[4,2,40960]{2,1,0:T(2,128)(2,1)}), bf16[4,2,40960]{2,1,0:T(2,128)(2,1)}, u32[]{:S(2)}, u32[]{:S(2)}) async-start(bf16[4,2,40960]{2,1,0:T(2,128)(2,1)} %reshape.661), calls=%async_computation.8 | async-start | bytes 1310720 | tf_op jit(solution)/shard_map/all_to_all | solution.py:265
  754.3 1.1 copy-start.24
  768.8 13.7 %all-to-all-start.8 = ((bf16[4,2,40960]{2,1,0:T(2,128)(2,1)}), bf16[4,2,40960]{2,1,0:T(2,128)(2,1)}, u32[]{:S(2)}, u32[]{:S(2)}) async-start(bf16[4,2,40960]{2,1,0:T(2,128)(2,1)} %reshape.663), calls=%async_computation.9 | async-start | bytes 1310720 | tf_op jit(solution)/shard_map/all_to_all | solution.py:266
Sparse Core Ops, SparseCore 0:
  202.1 138.1 all-reduce.5
  413.0 84.3 all-reduce.7
  501.3 193.5 all-reduce.9
Sparse Core Ops, SparseCore 1:
  200.5 36.7 all-gather.1
  506.6 56.6 reduce-scatter.1
where the time goes:
time: 808 us; the launch traced here: 795 us
  local copies, waits for them, and re-layouts  324 us (40%)
  waiting for transfers between devices  174 us (22%)
  other arithmetic  173 us (21%)
  starting transfers between devices  65.3 us (8%)
  matrix products  43.5 us (5%)
  between operations  16.2 us (2%)
    psum x1, waiting for transfers between devices, from_root(): return lax.psum(block, axis)  108 us
    unnamed x90, local copies, waits for them, and re-layouts  62.3 us
    unnamed x7, other arithmetic  53.9 us
    scatter-add x1, other arithmetic, per_device(): core = core.at[asked_block, :, :, asked_head, :].add(incoming)  50.5 us
    ppermute x2, waiting for transfers between devices, with_halo(): lax.ppermute(lax.slice_in_dim(block, 0, width, axis=dim), axis, backward)  43.6 us
    gather x3, local copies, waits for them, and re-layouts, per_device(): served = block_view[asked_block, :, :, asked_head, :]  40.8 us
    scatter x2, local copies, waits for them, and re-layouts, per_device(): outgoing = jnp.zeros((seq_count * capacity, block_len, 2, head_dim), jnp....  39.6 us
    reshape x2, local copies, waits for them, and re-layouts, per_device(): received.reshape(seq_count * capacity, block_len, 2, head_dim)[slot_of]  20.7 us
  transfers between devices with their start and end apart: 18, of which 6 were waited for; matrix products, arithmetic and copies ran while one was open for 58% of the time, Pallas kernels for 0%

commit v1 on v0

--- a/solution.py
+++ b/solution.py
@@ -23,7 +23,7 @@
 
 def from_root(block, axis, holder):
     block = jnp.where(lax.axis_index(axis) == holder, block, jnp.zeros_like(block))
-    return lax.psum(block, axis)
+    return jnp.sum(lax.all_gather(block, axis), axis=0)
 
 
 def per_device(queries, key_rows, values, rand_blocks, out_weight, cotangent):

time: 808 us -> 769 us (0.952)
  waiting for transfers between devices: 174 us -> 136 us
    psum x1 -> x0, waiting for transfers between devices: 108 us -> none  [from_root(): return lax.psum(block, axis)]
    all_gather x0 -> x1, waiting for transfers between devices: none -> 67.2 us  [from_root(): return jnp.sum(lax.all_gather(block, axis), axis=0)]
    unnamed x90 -> x88, local copies, waits for them, and re-layouts: 62.3 us -> 62.4 us
  transfers between devices with their start and end apart: 18 -> 18, of which waited for: 6 -> 6; matrix products, arithmetic and copies ran while one was open for 58% -> 61% of each run, Pallas kernels for 0% -> 0%
where the time goes in v1:
time: 769 us; the launch traced here: 757 us
  local copies, waits for them, and re-layouts  323 us (42%)
  other arithmetic  176 us (23%)
  waiting for transfers between devices  136 us (18%)
  starting transfers between devices  65.8 us (9%)
  matrix products  41 us (5%)
  between operations  15.1 us (2%)
    all_gather x1, waiting for transfers between devices, from_root(): return jnp.sum(lax.all_gather(block, axis), axis=0)  67.2 us
    unnamed x88, local copies, waits for them, and re-layouts  62.4 us
    unnamed x7, other arithmetic  54.4 us
    scatter-add x1, other arithmetic, per_device(): core = core.at[asked_block, :, :, asked_head, :].add(incoming)  50.8 us
    ppermute x2, waiting for transfers between devices, with_halo(): lax.ppermute(lax.slice_in_dim(block, 0, width, axis=dim), axis, backward)  45.9 us
    gather x3, local copies, waits for them, and re-layouts, per_device(): served = block_view[asked_block, :, :, asked_head, :]  40.9 us
    scatter x2, local copies, waits for them, and re-layouts, per_device(): outgoing = jnp.zeros((seq_count * capacity, block_len, 2, head_dim), jnp....  39.4 us
    ppermute x2, waiting for transfers between devices, with_halo(): lax.ppermute(lax.slice_in_dim(block, block.shape[dim] - width, None, axis...  21.1 us
  transfers between devices with their start and end apart: 18, of which 6 were waited for; matrix products, arithmetic and copies ran while one was open for 61% of the time, Pallas kernels for 0%

profile of v1, /device:TPU:38, one launch (start us, length us, event | category | flops | bytes accessed | tf_op | source)
XLA Modules:
  0.0 756.8 jit_solution(17509610031149775058)
XLA Ops:
  12.6 7.8 %all-to-all-start.3 = ((s32[16,1,15]{2,1,0:T(1,128)}), s32[16,1,15]{2,1,0:T(1,128)S(1)}, u32[]{:S(2)}, u32[]{:S(2)}) async-start(s32[16,1,15]{2,1,0:T(1,128)} %bitcast.20), calls=%async_computation.3 | async-start | bytes 16384 | tf_op jit(solution)/shard_map/all_to_all | solution.py:63
  20.4 5.9 copy.318
  26.8 12.6 %reduce.17 = bf16[2048,160]{1,0:T(8,128)(2,1)S(1)} reduce(bf16[2048,1,160]{2,1,0:T(2,128)(2,1)} %bitcast.314, bf16[]{:T(256)} %broadcast.542), dimensions={1}, to_apply=%bitcast.271.reduce_sub_computation | reduce | bytes 1310722
  41.8 4.5 all-to-all-start.1
  46.3 5.9 copy.315
  52.2 12.6 %reduce.18 = bf16[2048,160]{1,0:T(8,128)(2,1)S(1)} reduce(bf16[2048,1,160]{2,1,0:T(2,128)(2,1)} %bitcast.318, bf16[]{:T(256)} %broadcast.542), dimensions={1}, to_apply=%bitcast.273.reduce_sub_computation | reduce | bytes 1310722
  67.2 4.8 all-to-all-start
  72.7 5.9 copy.323
  78.5 12.6 %reduce.16 = bf16[2048,160]{1,0:T(8,128)(2,1)S(1)} reduce(bf16[2048,1,160]{2,1,0:T(2,128)(2,1)} %bitcast.319, bf16[]{:T(256)} %broadcast.542), dimensions={1}, to_apply=%bitcast.275.reduce_sub_computation | reduce | bytes 1310722
  93.6 4.2 reshape.655
  97.8 4.5 copy.319
  103.0 4.8 all-to-all-start.2
  107.8 4.2 reshape.657
  112.0 5.7 copy.316
  120.6 3.4 collective-permute-start
  127.5 5.5 collective-permute-done.1
  133.0 5.4 pad_maximum_fusion.6
  142.9 12.2 %gather_fusion = bf16[240,64,2,128]{3,1,2,0:T(8,128)(2,1)} fusion(bf16[10,64,2,4,128]{4,1,3,2,0:T(8,128)(2,1)S(1)} %copy.339, s32[240]{0:T(256)S(1)} %reshape.602), kind=kCustom, calls=%fused_computation | custom fusion | bytes 15730560 | tf_op jit(solution)/shard_map/gather | solution.py:68
  155.0 15.3 %copy.340 = bf16[240,64,2,128]{3,2,1,0:T(2,128)(2,1)} copy(bf16[240,64,2,128]{3,1,2,0:T(8,128)(2,1)} %gather_fusion) | data formatting | bytes 15728640 | tf_op jit(solution)/shard_map/gather | solution.py:68
  170.4 13.4 %gather.9 = bf16[16,15,64,256]{3,2,1,0:T(8,128)(2,1)} reshape(bf16[240,64,2,128]{3,2,1,0:T(2,128)(2,1)} %copy.340) | data formatting | bytes 15728640 | tf_op jit(solution)/shard_map/gather | solution.py:68
  183.8 7.0 broadcast_select_fusion.1
  190.8 6.6 all-to-all-start.4
  199.5 4.2 reshape.659
  203.8 5.7 copy.324
  218.4 3.9 stack.41
  224.1 4.9 pad_maximum_fusion.1
  230.1 3.6 select_reduce_fusion
  235.9 4.1 fusion.66
  241.7 67.2 %all-gather.6.cloned.1.call-done = bf16[1024,1024]{1,0:T(8,128)(2,1)} async-done(((bf16[64,1024]{1,0:T(8,128)(2,1)}), bf16[1024,1024]{1,0:T(8,128)(2,1)}) %all-gather.6.cloned.1.call-update) | async-done | bytes 2097168 | tf_op jit(solution)/shard_map/all_gather | solution.py:26
  315.0 12.1 %reshape.589 = bf16[240,64,2,128]{3,2,1,0:T(2,128)(2,1)} reshape(bf16[16,15,64,256]{3,2,1,0:T(8,128)(2,1)} %all-to-all-done.4) | data formatting | bytes 15728640 | tf_op jit(solution)/shard_map/reshape | solution.py:72
  327.1 8.5 %copy.341 = bf16[240,64,2,128]{3,1,2,0:T(8,128)(2,1)} copy(bf16[240,64,2,128]{3,2,1,0:T(2,128)(2,1)} %reshape.589) | data formatting | bytes 15728640 | tf_op jit(solution)/shard_map/reshape | solution.py:72
  335.6 11.1 %gather_fusion.1 = bf16[160,64,2,128]{3,1,2,0:T(8,128)(2,1)} fusion(bf16[240,64,2,128]{3,1,2,0:T(8,128)(2,1)} %copy.341, s32[1024]{0:T(1024)} %pad_clamp_fusion), kind=kCustom, calls=%fused_computation.1 | custom fusion | bytes 10486400 | tf_op jit(solution)/shard_map/gather | solution.py:72
  346.8 7.3 slice_bitcast_fusion.5
  377.3 3.9 fusion.17
  381.2 3.3 convert_bitcast_fusion
  392.0 4.2 copy.388
  396.2 5.1 broadcast_in_dim.101
  401.3 24.1 %scatter_fusion = bf16[240,64,2,128]{3,1,2,0:T(8,128)(2,1)} fusion(bf16[240,64,2,128]{3,1,2,0:T(8,128)(2,1)} %broadcast_in_dim.101, s32[160]{0:T(256)S(1)} %bitcast.347, bf16[160,64,2,128]{3,1,2,0:T(8,128)(2,1)} %copy.388), kind=kCustom, calls=%fused_computation.3 | custom fusion | bytes 15729280 | tf_op jit(solution)/shard_map/scatter | solution.py:250
  425.3 15.4 %copy.389 = bf16[240,64,2,128]{3,2,1,0:T(2,128)(2,1)} copy(bf16[240,64,2,128]{3,1,2,0:T(8,128)(2,1)} %scatter_fusion) | data formatting | bytes 15728640 | tf_op jit(solution)/shard_map/scatter | solution.py:250
  440.7 13.4 %reshape.599 = bf16[16,15,64,256]{3,2,1,0:T(8,128)(2,1)} reshape(bf16[240,64,2,128]{3,2,1,0:T(2,128)(2,1)} %copy.389) | data formatting | bytes 15728640 | tf_op jit(solution)/shard_map/reshape | solution.py:252
  454.1 7.3 all-to-all-start.6
  461.9 3.8 fusion.85
  481.1 3.8 fusion.14
  484.9 3.8 fusion.8
  495.7 5.4 collective-permute-start.2
  501.1 3.5 fusion.63
  507.5 5.6 reduce.19
  519.6 4.1 reshape.596
  524.0 40.4 %collective-permute-done.3 = bf16[64,1024]{1,0:T(8,128)(2,1)S(1)} collective-permute-done((bf16[64,1024]{1,0:T(8,128)(2,1)S(1)}, bf16[64,1024]{1,0:T(8,128)(2,1)S(1)}, u32[]{:S(2)}, u32[]{:S(2)}) %collective-permute-start.3) | collective-permute-done | bytes 131104 | tf_op jit(solution)/shard_map/ppermute | solution.py:19
  564.4 20.3 %collective-permute-done.2 = bf16[64,1024]{1,0:T(8,128)(2,1)S(1)} collective-permute-done((bf16[64,1024]{1,0:T(8,128)(2,1)S(1)}, bf16[64,1024]{1,0:T(8,128)(2,1)S(1)}, u32[]{:S(2)}, u32[]{:S(2)}) %collective-permute-start.2) | collective-permute-done | bytes 131104 | tf_op jit(solution)/shard_map/ppermute | solution.py:16
  587.2 4.2 reshape.598
  591.4 3.7 copy.390
  595.1 4.4 all-to-all-start.5
  599.5 16.2 %reshape.601 = f32[16,15,64,2,128]{4,3,2,1,0:T(2,128)} reshape(bf16[16,15,64,256]{3,2,1,0:T(8,128)(2,1)} %all-to-all-done.6) | data formatting | bytes 23592960 | tf_op jit(solution)/shard_map/convert_element_type | solution.py:256
  615.6 12.1 %broadcast_select_fusion = f32[16,15,64,2,128]{4,3,2,1,0:T(2,128)} fusion(f32[16,15,64,2,128]{4,3,2,1,0:T(2,128)} %reshape.601, pred[16,15]{1,0:T(8,128)(4,1)S(1)} %compare_bitcast_fusion), kind=kLoop, calls=%fused_computation.5 | loop fusion | flops 3932160 | bytes 31457520 | tf_op jit(solution)/shard_map/jit(_where)/select_n | solution.py:258
  627.8 13.4 %copy.391 = f32[240,64,2,128]{3,1,2,0:T(8,128)} copy(f32[240,64,2,128]{3,2,1,0:T(2,128)} %bitcast.299) | data formatting | bytes 31457280 | tf_op jit(solution)/shard_map/jit(_where)/select_n | solution.py:258
  641.1 50.8 %scatter_fusion.1 = f32[10,64,2,4,128]{4,1,3,2,0:T(8,128)} fusion(f32[10,64,2,4,128]{4,1,3,2,0:T(8,128)} %copy.390, s32[240]{0:T(256)S(1)} %reshape.632, f32[240,64,2,128]{3,1,2,0:T(8,128)} %copy.391), kind=kCustom, calls=%fused_computation.4 | custom fusion | flops 3932160 | bytes 47187840 | tf_op jit(solution)/shard_map/scatter-add | solution.py:259
  696.3 3.7 convert_element_type.103
  700.0 5.4 reduce.20
  708.4 5.2 all-to-all-start.7
  718.4 3.7 convert_element_type.104
  722.1 5.4 reduce.21
  730.5 4.8 all-to-all-start.8
  735.3 5.0 broadcast_multiply_fusion
  (217 shorter events, 139.0 us)
Async XLA Ops:
  7.2 228.8 %copy-start = (bf16[512,2048]{1,0:T(8,128)(2,1)S(1)}, bf16[512,2048]{1,0:T(8,128)(2,1)}, u32[]{:S(2)}) copy-start(bf16[512,2048]{1,0:T(8,128)(2,1)} %param.22) | copy-start | bytes 6291460
  10.8 188.1 %copy-start.30 = (s32[160,1]{0,1:T(1,128)}, s32[160,1]{0,1:T(1,128)S(1)}, u32[]{:S(2)}) copy-start(s32[160,1]{0,1:T(1,128)S(1)} %compare_select_fusion.2) | copy-start | bytes 1924
  12.6 29.2 %all-to-all-start.3 = ((s32[16,1,15]{2,1,0:T(1,128)}), s32[16,1,15]{2,1,0:T(1,128)S(1)}, u32[]{:S(2)}, u32[]{:S(2)}) async-start(s32[16,1,15]{2,1,0:T(1,128)} %bitcast.20), calls=%async_computation.3 | async-start | bytes 16384 | tf_op jit(solution)/shard_map/all_to_all | solution.py:63
  41.8 25.3 %all-to-all-start.1 = ((bf16[4,2,40960]{2,1,0:T(2,128)(2,1)}), bf16[4,2,40960]{2,1,0:T(2,128)(2,1)}, u32[]{:S(2)}, u32[]{:S(2)}) async-start(bf16[4,2,40960]{2,1,0:T(2,128)(2,1)} %reshape.654), calls=%async_computation.1 | async-start | bytes 1310720 | tf_op jit(solution)/shard_map/all_to_all | solution.py:37
  67.2 35.8 %all-to-all-start = ((bf16[4,2,40960]{2,1,0:T(2,128)(2,1)}), bf16[4,2,40960]{2,1,0:T(2,128)(2,1)}, u32[]{:S(2)}, u32[]{:S(2)}) async-start(bf16[4,2,40960]{2,1,0:T(2,128)(2,1)} %reshape.656), calls=%async_computation | async-start | bytes 1310720 | tf_op jit(solution)/shard_map/all_to_all | solution.py:36
  71.9 164.0 %all-gather.4.cloned.1.call-start = ((), (), s32[]{:S(2)}) async-start(), calls=%async_computation.11 | async-start | bytes 3276800 | tf_op jit(solution)/shard_map/all_gather | solution.py:143
  103.0 17.0 %copy-start.20 = (bf16[1,4,160,512]{3,2,1,0:T(8,128)(2,1)}, bf16[1,4,160,512]{3,2,1,0:T(8,128)(2,1)S(1)}, u32[]{:S(2)}) copy-start(bf16[1,4,160,512]{3,2,1,0:T(8,128)(2,1)S(1)} %copy.320) | copy-start | bytes 1966084
  103.0 87.8 %all-to-all-start.2 = ((bf16[4,2,40960]{2,1,0:T(2,128)(2,1)}), bf16[4,2,40960]{2,1,0:T(2,128)(2,1)}, u32[]{:S(2)}, u32[]{:S(2)}) async-start(bf16[4,2,40960]{2,1,0:T(2,128)(2,1)} %reshape.658), calls=%async_computation.2 | async-start | bytes 1310720 | tf_op jit(solution)/shard_map/all_to_all | solution.py:35
  120.6 6.8 collective-permute-start
  124.0 9.0 %collective-permute-start.1 = (bf16[64,1024]{1,0:T(8,128)(2,1)S(1)}, bf16[64,1024]{1,0:T(8,128)(2,1)S(1)}, u32[]{:S(2)}, u32[]{:S(2)}) collective-permute-start(bf16[64,1024]{1,0:T(8,128)(2,1)S(1)} %get-tuple-element.80), channel_id=1, source_target_pairs={{4,0},{8,4},{12,8},{16,12},{20,16},{24,20},{28,24},{32,28},{36,32}... | collective-permute-start | bytes 393224 | tf_op jit(solution)/shard_map/ppermute | solution.py:19
  138.4 1.1 copy-start.8
  190.8 124.3 %all-to-all-start.4 = ((bf16[16,15,64,256]{3,2,1,0:T(8,128)(2,1)}), bf16[16,15,64,256]{3,2,1,0:T(8,128)(2,1)}, u32[]{:S(2)}, u32[]{:S(2)}) async-start(bf16[16,15,64,256]{3,2,1,0:T(8,128)(2,1)} %broadcast_select_fusion.1), calls=%async_computation.4 | async-start | bytes 15728640 | tf_op jit(solution)/shard_map/all_to_all | solution.py:71
  197.4 111.6 %all-gather.6.cloned.1.call-start = ((), (), s32[]{:S(2)}) async-start(), calls=%async_computation.14 | async-start | bytes 2228224 | tf_op jit(solution)/shard_map/all_gather | solution.py:26
  198.1 290.5 %all-reduce.5.cloned.1.call-start = ((), (), s32[]{:S(2)}) async-start(), calls=%async_computation.12 | async-start | bytes 524288 | tf_op jit(solution)/shard_map/psum | solution.py:228
  209.5 7.2 copy-start.9
  218.4 3.9 copy-start.21
  229.0 1.1 copy-start.10
  230.1 3.6 copy-start.6
  241.7 132.4 %copy-start.2 = (bf16[10,64,4,128]{3,2,1,0:T(4,128)(2,1)}, bf16[10,64,4,128]{3,2,1,0:T(4,128)(2,1)S(1)}, u32[]{:S(2)}) copy-start(bf16[10,64,4,128]{3,2,1,0:T(4,128)(2,1)S(1)} %reshape.592) | copy-start | bytes 1966084
  354.1 0.9 copy-start.29
  355.0 6.9 copy-start.1
  355.0 3.6 copy-start.13
  356.5 3.2 copy-start.5
  365.0 1.0 copy-start.28
  365.0 1.6 copy-start.27
  369.9 0.8 copy-start.25
  371.5 363.8 %all-reduce.7.cloned.1.call-start = ((), (), s32[]{:S(2)}) async-start(), calls=%async_computation.13 | async-start | bytes 8388608 | tf_op jit(solution)/shard_map/psum | solution.py:149
  374.1 3.2 copy-start.18
  374.1 3.2 copy-start.23
  381.2 4.0 slice-start
  381.2 4.1 slice-start.1
  384.6 1.3 copy-start.3
  384.6 2.1 copy-start.17
  386.7 3.2 copy-start.11
  388.4 1.5 copy-start.14
  396.2 5.1 copy-start.31
  454.1 7.8 %copy-start.19 = (bf16[10,64,4,128]{3,2,1,0:T(4,128)(2,1)S(1)}, bf16[10,64,4,128]{3,2,1,0:T(4,128)(2,1)}, u32[]{:S(2)}) copy-start(bf16[10,64,4,128]{3,2,1,0:T(4,128)(2,1)} %copy.351) | copy-start | bytes 1966084
  454.1 141.0 %all-to-all-start.6 = ((bf16[16,15,64,256]{3,2,1,0:T(8,128)(2,1)}), bf16[16,15,64,256]{3,2,1,0:T(8,128)(2,1)}, u32[]{:S(2)}, u32[]{:S(2)}) async-start(bf16[16,15,64,256]{3,2,1,0:T(8,128)(2,1)} %reshape.599), calls=%async_computation.7 | async-start | bytes 15728640 | tf_op jit(solution)/shard_map/all_to_all | solution.py:254
  461.4 286.1 %reduce-scatter.2.cloned.1.call-start = ((), (), s32[]{:S(2)}) async-start(), calls=%async_computation.10 | async-start | bytes 6553600 | tf_op jit(solution)/shard_map/reduce_scatter | solution.py:137
  465.7 1.1 copy-start.4
  466.8 2.8 copy-start.7
  469.7 2.9 copy-start.12
  472.6 1.1 copy-start.22
  474.5 2.2 copy-start.26
  474.7 3.5 copy-start.15
  474.8 4.2 copy-start.16
  492.8 71.6 %collective-permute-start.3 = (bf16[64,1024]{1,0:T(8,128)(2,1)S(1)}, bf16[64,1024]{1,0:T(8,128)(2,1)S(1)}, u32[]{:S(2)}, u32[]{:S(2)}) collective-permute-start(bf16[64,1024]{1,0:T(8,128)(2,1)S(1)} %concatenate.44), channel_id=1, source_target_pairs={{4,0},{8,4},{12,8},{16,12},{20,16},{24,20},{28,24},{32,28},{36,32}... | collective-permute-start | bytes 393224 | tf_op jit(solution)/shard_map/ppermute | solution.py:19
  495.7 89.1 %collective-permute-start.2 = (bf16[64,1024]{1,0:T(8,128)(2,1)S(1)}, bf16[64,1024]{1,0:T(8,128)(2,1)S(1)}, u32[]{:S(2)}, u32[]{:S(2)}) collective-permute-start(bf16[64,1024]{1,0:T(8,128)(2,1)S(1)} %concatenate.43), channel_id=1, source_target_pairs={{0,4},{4,8},{8,12},{12,16},{16,20},{20,24},{24,28},{28,32},{32,36}... | collective-permute-start | bytes 393224 | tf_op jit(solution)/shard_map/ppermute | solution.py:16
  595.1 113.3 %all-to-all-start.5 = ((bf16[4,2,40960]{2,1,0:T(2,128)(2,1)}), bf16[4,2,40960]{2,1,0:T(2,128)(2,1)}, u32[]{:S(2)}, u32[]{:S(2)}) async-start(bf16[4,2,40960]{2,1,0:T(2,128)(2,1)} %reshape.660), calls=%async_computation.6 | async-start | bytes 1310720 | tf_op jit(solution)/shard_map/all_to_all | solution.py:264
  708.4 22.1 %all-to-all-start.7 = ((bf16[4,2,40960]{2,1,0:T(2,128)(2,1)}), bf16[4,2,40960]{2,1,0:T(2,128)(2,1)}, u32[]{:S(2)}, u32[]{:S(2)}) async-start(bf16[4,2,40960]{2,1,0:T(2,128)(2,1)} %reshape.662), calls=%async_computation.8 | async-start | bytes 1310720 | tf_op jit(solution)/shard_map/all_to_all | solution.py:265
  715.9 1.1 copy-start.24
  730.5 13.7 %all-to-all-start.8 = ((bf16[4,2,40960]{2,1,0:T(2,128)(2,1)}), bf16[4,2,40960]{2,1,0:T(2,128)(2,1)}, u32[]{:S(2)}, u32[]{:S(2)}) async-start(bf16[4,2,40960]{2,1,0:T(2,128)(2,1)} %reshape.664), calls=%async_computation.9 | async-start | bytes 1310720 | tf_op jit(solution)/shard_map/all_to_all | solution.py:266
Sparse Core Ops, SparseCore 0:
  74.4 37.5 all-gather.3
  200.9 108.0 all-gather.5
  371.6 84.1 all-reduce.4
  459.6 197.9 all-reduce.6
  659.8 57.0 reduce-scatter.1
